TPU v7x, 256 devices: a whole 4x4x8 slice. The times are simulated.
256 devices in a mesh: space: 32 (over x, z), sub: 8 (over y, core).
Axes of the slice: x: 4, y: 4, z: 8, core: 2. Of those that a mesh axis runs over, the one named last changes fastest.
Arguments:
- offsets: float32 [32, 8, 32, 8, 4, 3, 128], P('space', 'sub'), may hold values from 0.5 to 7.5
- normals: float32 [32, 8, 32, 8, 4, 3, 128], P('space', 'sub'), may hold values from -6 to 6
- density: float32 [32, 8, 32, 8, 4, 128], P('space', 'sub'), may hold values from 0.3 to 3
- tile_brick: int32 [32, 8, 32, 8, 4], P('space', 'sub'), may hold values from 0 to 63
- tile_count: int32 [32, 8, 32, 8, 4], P('space', 'sub'), may hold values from 32 to 128, as said below
Outputs:
- indicator: float32 [512, 128, 128], P('space', 'sub')
- density_field: float32 [512, 128, 128], P('space', 'sub')
Inputs may be any that keep to these rules, and one draw needn't show every extreme that they name: `tile_count`: slots at and beyond a tile's count are padding; some tile holds 128 live points.
All inputs are finite; a program needn't handle non-finite values.
Results may differ from a plain program's by a relative error of at most 0.0003.
Values sent between devices are 32-bit elements; how exact they have to be, the bound alone decides.
No kernel may reach another device: no remote copies, remote signals or barrier semaphores. Data moves between devices by JAX's collectives and lax.ppermute only.
A program may use at most 192 MiB of HBM per device.

v0:
```python
import math

import jax
import jax.numpy as jnp
from jax import lax
from jax.sharding import PartitionSpec as P

BRICK = 8
CX = 16
CY = 16
CZ = 128
LEVELS = 4
SWEEPS = 2
COARSE = 8


screen_weight = 0.05
relax_weight = 0.8


def with_halo(x, sides, width):
    for axis, dim in sides:
        devices, length = (lax.axis_size(axis), x.shape[dim])
        up = [(i, (i + 1) % devices) for i in range(devices - 1)]
        down = [(j, i) for i, j in up]
        last = lax.slice_in_dim(x, length - width, length, axis=dim)
        first = lax.slice_in_dim(x, 0, width, axis=dim)
        before = lax.ppermute(last, axis, up)
        after = lax.ppermute(first, axis, down)
        x = jnp.concatenate([before, x, after], axis=dim)
    return x


def splat_tiles(offsets_tile, samples_tile):
    tile_total = offsets_tile.shape[0]
    slot_total = offsets_tile.shape[2]
    centers = jnp.arange(BRICK, dtype=jnp.float32) + 0.5
    weights = jnp.maximum(
        0.0, 1.0 - jnp.abs(offsets_tile[:, :, None, :] - centers[None, None, :, None])
    )
    planar = (weights[:, 0, :, None, :] * weights[:, 1, None, :, :]).reshape(
        tile_total, BRICK * BRICK, slot_total
    )
    loaded = (samples_tile[:, :, None, :] * weights[:, 2][:, None, :, :]).reshape(
        tile_total, 4 * BRICK, slot_total
    )
    result = jnp.einsum("tas,tbs->tab", planar, loaded, precision=lax.Precision.HIGHEST)
    return result.reshape(tile_total, -1)


def splat_blocks(offsets_flat, samples_flat):
    tile_total = offsets_flat.shape[0]
    block_size = math.gcd(tile_total, 64)
    slot_total = offsets_flat.shape[2]

    def one_block(inputs):
        return splat_tiles(inputs[0], inputs[1])

    result = lax.map(
        one_block,
        (
            offsets_flat.reshape(tile_total // block_size, block_size, 3, slot_total),
            samples_flat.reshape(tile_total // block_size, block_size, 4, slot_total),
        ),
    )
    return result.reshape(tile_total, -1)


def to_grid(sums):
    shaped = sums.reshape(CX // BRICK, CY // BRICK, CZ // BRICK, BRICK, BRICK, 4, BRICK)
    return shaped.transpose(5, 0, 3, 1, 4, 2, 6).reshape(4, CX, CY, CZ)


def neighbours(padded):
    total = padded[2:, 1:-1, 1:-1] + padded[:-2, 1:-1, 1:-1]
    total = total + padded[1:-1, 2:, 1:-1] + padded[1:-1, :-2, 1:-1]
    return total + padded[1:-1, 1:-1, 2:] + padded[1:-1, 1:-1, :-2]


def operate(padded, field, screen, level_index):
    return (6.0 * field - neighbours(padded)) * 0.25**level_index + screen * field


def pad_shared(field):
    rimmed = with_halo(field, (("space", 0), ("sub", 1)), 1)
    return jnp.pad(rimmed, ((0, 0), (0, 0), (1, 1)))


def sweep(padded, field, forcing, screen, diagonal, level_index):
    return field + relax_weight * (forcing - operate(padded, field, screen, level_index)) / diagonal


def restrict(field):
    sx, sy, sz = field.shape
    return field.reshape(sx // 2, 2, sy // 2, 2, sz // 2, 2).mean(axis=(1, 3, 5))


def prolong(field):
    return jnp.repeat(jnp.repeat(jnp.repeat(field, 2, axis=0), 2, axis=1), 2, axis=2)


def single_action(field, action, forcing, screen, diagonal, level_index):
    padded = pad_shared(field)
    if action == "residual":
        return (field, forcing - operate(padded, field, screen, level_index))
    return (sweep(padded, field, forcing, screen, diagonal, level_index), None)


def apply_actions(field, actions, forcing, screen, diagonal, level_index):
    residual = None
    position = 0
    while position < len(actions):
        field, residual = single_action(
            field, actions[position], forcing, screen, diagonal, level_index
        )
        position = position + 1
    return (field, residual)


def coarsest_solve(forcing, screen, level_index):
    diagonal = 6.0 * 0.25**level_index + screen
    field = relax_weight * forcing / diagonal
    field, unused = apply_actions(
        field, ["sweep"] * (COARSE - 1), forcing, screen, diagonal, level_index
    )
    return field


def vcycle(forcing, level_index, screens):
    screen = screens[level_index]
    if level_index == LEVELS - 1:
        return coarsest_solve(forcing, screen, level_index)
    diagonal = 6.0 * 0.25**level_index + screen
    field = relax_weight * forcing / diagonal
    field, residual = apply_actions(
        field, ["sweep"] * (SWEEPS - 1) + ["residual"], forcing, screen, diagonal, level_index
    )
    correction = vcycle(restrict(residual), level_index + 1, screens)
    field = field + prolong(correction)
    field, unused = apply_actions(field, ["sweep"] * SWEEPS, forcing, screen, diagonal, level_index)
    return field


def on_device(offsets, normals, density, tile_brick, tile_count):
    space_count = lax.axis_size("space")
    sub_count = lax.axis_size("sub")
    tiles_each = offsets.shape[4]
    slot_total = offsets.shape[6]
    brick_total = CX // BRICK * (CY // BRICK) * (CZ // BRICK)
    offsets_local = offsets.reshape(space_count, sub_count, tiles_each, 3, slot_total)
    samples = jnp.concatenate(
        [
            normals.reshape(space_count, sub_count, tiles_each, 3, slot_total),
            density.reshape(space_count, sub_count, tiles_each, 1, slot_total),
        ],
        axis=3,
    )
    slot_numbers = lax.broadcasted_iota(
        jnp.int32, (space_count, sub_count, tiles_each, slot_total), 3
    )
    live_slots = (
        slot_numbers < tile_count.reshape(space_count, sub_count, tiles_each)[..., None]
    ).astype(jnp.float32)
    samples = samples * live_slots[:, :, :, None, :]
    brick_ids = tile_brick.reshape(space_count, sub_count, tiles_each).astype(jnp.float32)
    partials_out = splat_blocks(
        offsets_local.reshape(-1, 3, slot_total), samples.reshape(-1, 4, slot_total)
    )
    partials_out = partials_out.reshape(space_count, sub_count, tiles_each, -1)
    partials_in, brick_in = (
        lax.all_to_all(
            lax.all_to_all(partials_out, "space", split_axis=0, concat_axis=0, tiled=True),
            "sub",
            split_axis=1,
            concat_axis=1,
            tiled=True,
        ),
        lax.all_to_all(
            lax.all_to_all(brick_ids, "space", split_axis=0, concat_axis=0, tiled=True),
            "sub",
            split_axis=1,
            concat_axis=1,
            tiled=True,
        ),
    )
    partials = partials_in.reshape(space_count * sub_count * tiles_each, -1)
    brick_numbers = jnp.arange(brick_total, dtype=jnp.float32)
    onehot = (brick_in.reshape(-1)[None, :] == brick_numbers[:, None]).astype(jnp.float32)
    sums = jnp.dot(
        onehot, partials, precision=lax.Precision.HIGHEST, preferred_element_type=jnp.float32
    )
    grid = to_grid(sums)
    density_field = grid[3]
    padded_x = with_halo(grid[0], (("space", 0),), 1)
    padded_y = with_halo(grid[1], (("sub", 1),), 1)
    padded_z = jnp.pad(grid[2], ((0, 0), (0, 0), (1, 1)))
    change = padded_x[2:] - padded_x[:-2] + (padded_y[:, 2:] - padded_y[:, :-2])
    change = change + (padded_z[:, :, 2:] - padded_z[:, :, :-2])
    forcing = -0.5 * change
    screens = []
    rho_level = density_field
    for level_index in range(LEVELS):
        screens.append(screen_weight * rho_level)
        rho_level = restrict(rho_level) if level_index < LEVELS - 1 else rho_level
    indicator = vcycle(forcing, 0, screens)
    return (indicator, density_field)


def solution(mesh):
    placed = (
        P("space", "sub", None, None, None, None, None),
        P("space", "sub", None, None, None, None, None),
        P("space", "sub", None, None, None, None),
        P("space", "sub", None, None, None),
        P("space", "sub", None, None, None),
    )
    return jax.shard_map(
        on_device,
        mesh=mesh,
        in_specs=placed,
        out_specs=(P("space", "sub", None), P("space", "sub", None)),
        check_vma=False,
    )
```

profile of v0, /device:TPU:14, one launch (start us, length us, event | category | flops | bytes accessed | tf_op | source)
XLA Modules:
  0.0 880.5 jit_solution(2987007734797802999)
XLA Ops:
  2.1 11.6 %all-to-all-start = ((f32[32,8,4]{1,2,0:T(4,128)}), f32[32,8,4]{1,2,0:T(4,128)S(1)}, u32[]{:S(2)}, u32[]{:S(2)}) async-start(f32[32,8,4]{1,2,0:T(4,128)} %convert_bitcast_fusion), calls=%async_computation | async-start | bytes 131072 | tf_op jit(solution)/shard_map/all_to_all | solution.py:179
  22.5 124.0 %while.10 = (s32[]{:T(128)}, f32[16,64,2048]{2,1,0:T(8,128)}, f32[16,64,3,128]{3,1,0,2:T(8,128)}, f32[16,64,4,128]{3,2,1,0:T(4,128)}, s32[]{:T(128)}) while((s32[]{:T(128)}, f32[16,64,2048]{2,1,0:T(8,128)}, f32[16,64,3,128]{3,1,0,2:T(8,128)}, f32[16,64,4,128]{3,2,1,0:T(4,128)}, s32[]{:T(128)}) %tuple.80), condition=%wide.region_1.2_spmd, body=%wide.region_0.1_spmd.sunk | while | flops 202899472 | bytes 7504517 | solution.py:59
  24.6 3.4 fusion.215
  40.2 3.4 fusion.215
  47.9 3.4 fusion.215
  55.6 3.4 fusion.215
  63.4 3.4 fusion.215
  71.1 3.4 fusion.215
  78.8 3.4 fusion.215
  86.6 3.4 fusion.215
  146.6 9.8 %reshape_reshape.4 = f32[32,8,4,2048]{3,2,1,0:T(4,128)} reshape(f32[16,64,2048]{2,1,0:T(8,128)} %get-tuple-element.24) | data formatting | bytes 16777216 | tf_op jit(solution)/shard_map/reshape;reshape | solution.py:169
  156.4 9.8 %all-to-all-start.2 = ((f32[32,8,4,2048]{3,2,1,0:T(4,128)}), f32[32,8,4,2048]{3,2,1,0:T(4,128)}, u32[]{:S(2)}, u32[]{:S(2)}) async-start(f32[32,8,4,2048]{3,2,1,0:T(4,128)} %reshape_reshape.4), calls=%async_computation.2 | async-start | bytes 16777216 | tf_op jit(solution)/shard_map/all_to_all | solution.py:172
  167.0 184.1 %all-to-all-done.2 = f32[32,8,4,2048]{3,2,1,0:T(4,128)} async-done(((f32[32,8,4,2048]{3,2,1,0:T(4,128)}), f32[32,8,4,2048]{3,2,1,0:T(4,128)}, u32[]{:S(2)}, u32[]{:S(2)}) %all-to-all-start.2) | async-done | bytes 8388640 | tf_op jit(solution)/shard_map/all_to_all | solution.py:172
  351.0 4.9 all-to-all-start.1
  356.0 10.5 %copy.204 = f32[32,8,4,2048]{3,2,0,1:T(4,128)} copy(f32[32,8,4,2048]{3,2,1,0:T(4,128)} %all-to-all-done.2) | data formatting | bytes 16777216 | tf_op jit(solution)/shard_map/all_to_all | solution.py:172
  366.4 5.4 all-to-all-start.3
  373.3 91.7 %all-to-all-done.3 = f32[32,8,4,2048]{3,2,0,1:T(4,128)} async-done(((f32[32,8,4,2048]{3,2,0,1:T(4,128)}), f32[32,8,4,2048]{3,2,0,1:T(4,128)}, u32[]{:S(2)}, u32[]{:S(2)}) %all-to-all-start.3) | async-done | bytes 8388640 | tf_op jit(solution)/shard_map/all_to_all | solution.py:171
  465.0 10.5 %copy.205 = f32[32,8,4,2048]{3,2,1,0:T(4,128)} copy(f32[32,8,4,2048]{3,2,0,1:T(4,128)} %all-to-all-done.3) | data formatting | bytes 16777216 | tf_op jit(solution)/shard_map/all_to_all | solution.py:171
  475.4 10.0 %reshape.123 = f32[1024,2048]{1,0:T(8,128)} reshape(f32[32,8,4,2048]{3,2,1,0:T(4,128)} %copy.205) | data formatting | bytes 16777216 | tf_op jit(solution)/shard_map/reshape | solution.py:186
  485.5 9.3 %copy.206 = f32[2048,1024]{1,0:T(8,128)} copy(f32[2048,1024]{0,1:T(8,128)} %bitcast.74) | data formatting | bytes 16777216 | tf_op jit(solution)/shard_map/dot_general | solution.py:189
  494.7 9.4 %convolution_bitcast_fusion = f32[4,2,8,2,8,16,8]{5,6,0,4,2,3,1:T(8,128)S(1)} fusion(f32[8,8,4,8,1024,1,1]{4,3,2,1,0,6,5:T(8,128)} %bitcast.76, f32[2,2,16]{2,1,0:T(2,128)S(1)} %multiply_add_fusion, f32[1024]{0:T(1024)S(1)} %eq.32), kind=kOutput, calls=%fused_computation.17 | convolution fusion | flops 1610678272 | bytes 8917248 | tf_op jit(solution)/shard_map/dot_general | solution.py:189
  509.6 8.2 collective-permute-start
  536.1 6.0 collective-permute-start.4
  544.1 5.7 collective-permute-done.5
  559.5 3.9 collective-permute-start.9
  563.4 3.7 collective-permute-done.9
  571.5 4.4 reshape_squeeze.3
  575.9 4.0 reduce_sum.55
  580.3 9.8 %reshape.124 = f32[8,2,8,2,64,2]{5,4,3,2,1,0:T(8,128)} reshape(f32[16,16,128]{2,1,0:T(8,128)S(1)} %fusion.35) | data formatting | bytes 262144 | tf_op jit(solution)/shard_map/reshape | solution.py:95
  590.1 4.0 reduce_sum.54
  596.1 3.9 collective-permute-start.13
  600.0 3.7 collective-permute-done.13
  612.9 3.9 collective-permute-start.17
  616.8 3.7 collective-permute-done.17
  630.7 3.9 collective-permute-start.21
  634.7 3.6 collective-permute-done.21
  647.3 3.9 collective-permute-start.25
  651.2 3.6 collective-permute-done.25
  664.1 3.9 collective-permute-start.29
  668.0 3.6 collective-permute-done.29
  680.6 3.9 collective-permute-start.33
  684.6 3.6 collective-permute-done.33
  697.1 3.9 collective-permute-start.37
  701.1 3.6 collective-permute-done.37
  713.7 3.9 collective-permute-start.41
  717.6 3.6 collective-permute-done.41
  730.2 3.9 collective-permute-start.45
  734.1 3.6 collective-permute-done.45
  746.7 4.1 collective-permute-start.49
  750.9 3.4 collective-permute-done.49
  763.3 3.9 collective-permute-start.53
  767.2 3.6 collective-permute-done.53
  780.0 3.9 collective-permute-start.57
  784.0 3.6 collective-permute-done.57
  796.6 3.9 collective-permute-start.61
  800.5 3.6 collective-permute-done.61
  813.5 3.9 collective-permute-start.65
  817.4 3.7 collective-permute-done.65
  830.1 3.9 collective-permute-start.69
  834.0 3.7 collective-permute-done.69
  847.6 3.9 collective-permute-start.73
  851.6 3.7 collective-permute-done.73
  864.6 3.9 collective-permute-start.77
  868.5 3.7 collective-permute-done.77
  (406 shorter events, 305.0 us)
Async XLA Ops:
  2.1 154.2 %all-to-all-start = ((f32[32,8,4]{1,2,0:T(4,128)}), f32[32,8,4]{1,2,0:T(4,128)S(1)}, u32[]{:S(2)}, u32[]{:S(2)}) async-start(f32[32,8,4]{1,2,0:T(4,128)} %convert_bitcast_fusion), calls=%async_computation | async-start | bytes 131072 | tf_op jit(solution)/shard_map/all_to_all | solution.py:179
  156.4 194.7 %all-to-all-start.2 = ((f32[32,8,4,2048]{3,2,1,0:T(4,128)}), f32[32,8,4,2048]{3,2,1,0:T(4,128)}, u32[]{:S(2)}, u32[]{:S(2)}) async-start(f32[32,8,4,2048]{3,2,1,0:T(4,128)} %reshape_reshape.4), calls=%async_computation.2 | async-start | bytes 16777216 | tf_op jit(solution)/shard_map/all_to_all | solution.py:172
  351.0 15.4 %all-to-all-start.1 = ((f32[8,1,128]{2,1,0:T(1,128)}), f32[8,1,128]{2,1,0:T(1,128)S(1)}, u32[]{:S(2)}, u32[]{:S(2)}) async-start(f32[8,1,128]{2,1,0:T(1,128)} %reshape.138), calls=%async_computation.1 | async-start | bytes 8192 | tf_op jit(solution)/shard_map/all_to_all | solution.py:178
  366.4 98.6 %all-to-all-start.3 = ((f32[32,8,4,2048]{3,2,0,1:T(4,128)}), f32[32,8,4,2048]{3,2,0,1:T(4,128)}, u32[]{:S(2)}, u32[]{:S(2)}) async-start(f32[32,8,4,2048]{3,2,0,1:T(4,128)} %copy.204), calls=%async_computation.3 | async-start | bytes 16777216 | tf_op jit(solution)/shard_map/all_to_all | solution.py:171
  509.6 25.6 %collective-permute-start = (f32[1,16,128]{2,1,0:T(8,128)}, f32[1,16,128]{2,1,0:T(8,128)S(1)}, u32[]{:S(2)}, u32[]{:S(2)}) collective-permute-start(f32[1,16,128]{2,1,0:T(8,128)} %get-tuple-element.78), channel_id=1, source_target_pairs={{8,0},{16,8},{24,16},{32,24},{40,32},{48,40},{56,48},{64,56},{72,6... | collective-permute-start | bytes 24584 | tf_op jit(solution)/shard_map/ppermute | solution.py:29
  517.7 17.5 %collective-permute-start.1 = (f32[1,16,128]{2,1,0:T(8,128)}, f32[1,16,128]{2,1,0:T(8,128)S(1)}, u32[]{:S(2)}, u32[]{:S(2)}) collective-permute-start(f32[1,16,128]{2,1,0:T(8,128)} %get-tuple-element.79), channel_id=1, source_target_pairs={{0,8},{8,16},{16,24},{24,32},{32,40},{40,48},{48,56},{56,64},{64,7... | collective-permute-start | bytes 24584 | tf_op jit(solution)/shard_map/ppermute | solution.py:28
  523.2 12.0 %collective-permute-start.2 = (f32[16,1,128]{2,1,0:T(1,128)}, f32[16,1,128]{2,1,0:T(1,128)}, u32[]{:S(2)}, u32[]{:S(2)}) collective-permute-start(f32[16,1,128]{2,1,0:T(1,128)} %get-tuple-element.80), channel_id=1, source_target_pairs={{1,0},{2,1},{3,2},{4,3},{5,4},{6,5},{7,6},{9,8},{10,9},{11,10},{12... | collective-permute-start | bytes 24584 | tf_op jit(solution)/shard_map/ppermute | solution.py:29
  525.4 9.8 %collective-permute-start.3 = (f32[16,1,128]{2,1,0:T(1,128)}, f32[16,1,128]{2,1,0:T(1,128)}, u32[]{:S(2)}, u32[]{:S(2)}) collective-permute-start(f32[16,1,128]{2,1,0:T(1,128)} %get-tuple-element.81), channel_id=1, source_target_pairs={{0,1},{1,2},{2,3},{3,4},{4,5},{5,6},{6,7},{8,9},{9,10},{10,11},{11... | collective-permute-start | bytes 24584 | tf_op jit(solution)/shard_map/ppermute | solution.py:28
  536.1 8.0 collective-permute-start.4
  542.1 7.7 collective-permute-start.5
  551.7 5.4 collective-permute-start.7
  557.5 5.9 collective-permute-start.8
  559.5 7.7 collective-permute-start.9
  567.1 12.8 %collective-permute-start.10 = (f32[18,1,128]{2,1,0:T(1,128)S(1)}, f32[18,1,128]{2,1,0:T(1,128)S(1)}, u32[]{:S(2)}, u32[]{:S(2)}) collective-permute-start(f32[18,1,128]{2,1,0:T(1,128)S(1)} %get-tuple-element.67), channel_id=1, source_target_pairs={{1,0},{2,1},{3,2},{4,3},{5,4},{6,5},{7,6},{9,8},{10,9},{11,10},{12... | collective-permute-start | bytes 27656 | tf_op jit(solution)/shard_map/ppermute | solution.py:29
  569.1 10.8 %collective-permute-start.11 = (f32[18,1,128]{2,1,0:T(1,128)S(1)}, f32[18,1,128]{2,1,0:T(1,128)S(1)}, u32[]{:S(2)}, u32[]{:S(2)}) collective-permute-start(f32[18,1,128]{2,1,0:T(1,128)S(1)} %get-tuple-element.66), channel_id=1, source_target_pairs={{0,1},{1,2},{2,3},{3,4},{4,5},{5,6},{6,7},{8,9},{9,10},{10,11},{11... | collective-permute-start | bytes 27656 | tf_op jit(solution)/shard_map/ppermute | solution.py:28
  594.2 5.9 collective-permute-start.12
  596.1 7.6 collective-permute-start.13
  605.7 4.9 collective-permute-start.15
  610.9 5.9 collective-permute-start.16
  612.9 7.6 collective-permute-start.17
  620.5 5.6 collective-permute-start.18
  622.4 4.9 collective-permute-start.19
  628.8 5.9 collective-permute-start.20
  630.7 7.6 collective-permute-start.21
  640.3 4.9 collective-permute-start.23
  645.4 5.9 collective-permute-start.24
  647.3 7.6 collective-permute-start.25
  656.8 4.9 collective-permute-start.27
  662.2 5.9 collective-permute-start.28
  664.1 7.6 collective-permute-start.29
  678.7 5.9 collective-permute-start.32
  680.6 7.6 collective-permute-start.33
  690.1 4.9 collective-permute-start.35
  695.2 5.9 collective-permute-start.36
  697.1 7.6 collective-permute-start.37
  706.7 4.9 collective-permute-start.39
  711.7 5.9 collective-permute-start.40
  713.7 7.6 collective-permute-start.41
  723.2 4.9 collective-permute-start.43
  728.3 5.9 collective-permute-start.44
  730.2 7.6 collective-permute-start.45
  739.7 4.9 collective-permute-start.47
  744.8 6.1 collective-permute-start.48
  746.7 7.6 collective-permute-start.49
  761.3 5.9 collective-permute-start.52
  763.3 7.6 collective-permute-start.53
  778.1 5.9 collective-permute-start.56
  780.0 7.6 collective-permute-start.57
  789.6 4.9 collective-permute-start.59
  794.7 5.9 collective-permute-start.60
  796.6 7.6 collective-permute-start.61
  806.1 4.9 collective-permute-start.63
  811.5 5.9 collective-permute-start.64
  813.5 7.6 collective-permute-start.65
  823.0 4.9 collective-permute-start.67
  828.2 5.9 collective-permute-start.68
  830.1 7.6 collective-permute-start.69
  839.6 4.9 collective-permute-start.71
  845.7 5.9 collective-permute-start.72
  847.6 7.7 collective-permute-start.73
  857.2 5.0 collective-permute-start.75
  862.6 5.9 collective-permute-start.76
  864.6 7.7 collective-permute-start.77
  874.2 5.0 collective-permute-start.79
  (22 other events, 457.1 us)
where the time goes:
time: 892 us; the launch traced here: 880 us
  waiting for transfers between devices  391 us (44%)
  starting transfers between devices  242 us (27%)
  local copies, waits for them, and re-layouts  159 us (18%)
  matrix products  63.6 us (7%)
  other arithmetic  21.8 us (2%)
    all_to_all x1, waiting for transfers between devices, on_device(): lax.all_to_all(partials_out, 'space', split_axis=0, concat_axis=0, tiled=...  184 us
    ppermute x40, starting transfers between devices, with_halo(): before = lax.ppermute(last, axis, up)  123 us
    ppermute x40, waiting for transfers between devices, with_halo(): before = lax.ppermute(last, axis, up)  115 us
    all_to_all x1, waiting for transfers between devices, on_device(): lax.all_to_all(lax.all_to_all(partials_out, 'space', split_axis=0, concat...  91.7 us
    ppermute x40, starting transfers between devices, with_halo(): after = lax.ppermute(first, axis, down)  87.6 us
    dot_general x16, matrix products, splat_tiles(): jnp.einsum('tas,tbs->tab', planar, loaded, precision=lax.Precision.HIGHEST)  54.2 us
    dynamic_update_slice x32, local copies, waits for them, and re-layouts, splat_blocks(): lax.map(one_block, (offsets_flat.reshape(tile_total // block_size, block_...  18.8 us
  transfers between devices with their start and end apart: 84, of which 39 were waited for; matrix products, arithmetic and copies ran while one was open for 20% of the time, Pallas kernels for 0%

commit v1 on v0

v1 whole, which is shorter than its diff:
```python
import jax
import jax.numpy as jnp
from jax import lax
from jax.sharding import PartitionSpec as P

BRICK = 8
CX = 16
CY = 16
CZ = 128
LEVELS = 4
SWEEPS = 2
COARSE = 8

screen_weight = 0.05
relax_weight = 0.8

HALO0 = 4
HALO1 = 4


def exchange(x, width, dim_x, dim_y):
    for axis, dim in (("space", dim_x), ("sub", dim_y)):
        devices = lax.axis_size(axis)
        length = x.shape[dim]
        up = [(i, i + 1) for i in range(devices - 1)]
        down = [(j, i) for i, j in up]
        last = lax.slice_in_dim(x, length - width, length, axis=dim)
        first = lax.slice_in_dim(x, 0, width, axis=dim)
        before = lax.ppermute(last, axis, up)
        after = lax.ppermute(first, axis, down)
        x = jnp.concatenate([before, x, after], axis=dim)
    return x


def crop(x, h_from, h_to):
    d = h_from - h_to
    if d == 0:
        return x
    return x[d:-d, d:-d]


def inside_mask(nx, ny, nz, halo):
    dev_x = lax.axis_index("space")
    dev_y = lax.axis_index("sub")
    total_x = lax.axis_size("space") * nx
    total_y = lax.axis_size("sub") * ny
    gx = lax.broadcasted_iota(jnp.int32, (nx + 2 * halo, ny + 2 * halo, nz), 0) + dev_x * nx - halo
    gy = lax.broadcasted_iota(jnp.int32, (nx + 2 * halo, ny + 2 * halo, nz), 1) + dev_y * ny - halo
    ok = (gx >= 0) & (gx < total_x) & (gy >= 0) & (gy < total_y)
    return ok.astype(jnp.float32)


def operate_ext(u, screen_c, scale):
    c = u[1:-1, 1:-1, :]
    zp = jnp.pad(c, ((0, 0), (0, 0), (1, 1)))
    total = u[2:, 1:-1] + u[:-2, 1:-1]
    total = total + u[1:-1, 2:] + u[1:-1, :-2]
    total = total + zp[:, :, 2:] + zp[:, :, :-2]
    return (6.0 * c - total) * scale + screen_c * c


def sweep_ext(u, h, f, screen, diag, mask, scale):
    fc, sc, dc = crop(f, h, h - 1), crop(screen, h, h - 1), crop(diag, h, h - 1)
    new = crop(u, h, h - 1) + relax_weight * (fc - operate_ext(u, sc, scale)) / dc
    return new * crop(mask, h, h - 1)


def restrict(field):
    sx, sy, sz = field.shape
    return field.reshape(sx // 2, 2, sy // 2, 2, sz // 2, 2).mean(axis=(1, 3, 5))


def prolong(field):
    return jnp.repeat(jnp.repeat(jnp.repeat(field, 2, axis=0), 2, axis=1), 2, axis=2)


def neighbours(padded):
    total = padded[2:, 1:-1, 1:-1] + padded[:-2, 1:-1, 1:-1]
    total = total + padded[1:-1, 2:, 1:-1] + padded[1:-1, :-2, 1:-1]
    return total + padded[1:-1, 1:-1, 2:] + padded[1:-1, 1:-1, :-2]


def operate(field, screen, level_index):
    return (6.0 * field - neighbours(jnp.pad(field, 1))) * (0.25**level_index) + screen * field


def sweep(field, forcing, screen, diagonal, level_index):
    return field + relax_weight * (forcing - operate(field, screen, level_index)) / diagonal


def vcycle_global(forcing, level_index, screens):
    screen = screens[level_index]
    diagonal = 6.0 * (0.25**level_index) + screen
    field = relax_weight * forcing / diagonal
    if level_index == LEVELS - 1:
        for _ in range(COARSE - 1):
            field = sweep(field, forcing, screen, diagonal, level_index)
        return field
    for _ in range(SWEEPS - 1):
        field = sweep(field, forcing, screen, diagonal, level_index)
    residual = forcing - operate(field, screen, level_index)
    correction = vcycle_global(restrict(residual), level_index + 1, screens)
    field = field + prolong(correction)
    for _ in range(SWEEPS):
        field = sweep(field, forcing, screen, diagonal, level_index)
    return field


def splat(packed):
    tiles, _, slots = packed.shape
    offsets = packed[:, 0:3, :]
    samples = packed[:, 3:7, :]
    bricks = packed[:, 7, 0].astype(jnp.int32)
    centers = jnp.arange(BRICK, dtype=jnp.float32) + 0.5
    weights = jnp.maximum(0.0, 1.0 - jnp.abs(offsets[:, :, None, :] - centers[None, None, :, None]))
    planar = (weights[:, 0, :, None, :] * weights[:, 1, None, :, :]).reshape(
        tiles, BRICK * BRICK, slots
    )
    loaded = (samples[:, :, None, :] * weights[:, 2][:, None, :, :]).reshape(
        tiles, 4 * BRICK, slots
    )
    partials = jnp.einsum("tas,tbs->tab", planar, loaded, precision=lax.Precision.HIGHEST)
    partials = partials.reshape(tiles, -1)
    brick_total = CX // BRICK * (CY // BRICK) * (CZ // BRICK)
    onehot = (bricks[None, :] == jnp.arange(brick_total, dtype=jnp.int32)[:, None]).astype(
        jnp.float32
    )
    return jnp.dot(
        onehot, partials, precision=lax.Precision.HIGHEST, preferred_element_type=jnp.float32
    )


def to_grid(sums):
    shaped = sums.reshape(CX // BRICK, CY // BRICK, CZ // BRICK, BRICK, BRICK, 4, BRICK)
    return shaped.transpose(5, 0, 3, 1, 4, 2, 6).reshape(4, CX, CY, CZ)


def on_device(offsets, normals, density, tile_brick, tile_count):
    space_count = lax.axis_size("space")
    sub_count = lax.axis_size("sub")
    devices = space_count * sub_count
    tiles_each = offsets.shape[4]
    slot_total = offsets.shape[6]

    slot_numbers = lax.broadcasted_iota(jnp.int32, (devices, tiles_each, 1, slot_total), 3)
    live = (slot_numbers < tile_count.reshape(devices, tiles_each, 1, 1)).astype(jnp.float32)
    samples = jnp.concatenate(
        [
            normals.reshape(devices, tiles_each, 3, slot_total),
            density.reshape(devices, tiles_each, 1, slot_total),
        ],
        axis=2,
    ) * live
    brick_row = jnp.broadcast_to(
        tile_brick.reshape(devices, tiles_each, 1, 1).astype(jnp.float32),
        (devices, tiles_each, 1, slot_total),
    )
    packed = jnp.concatenate(
        [offsets.reshape(devices, tiles_each, 3, slot_total), samples, brick_row], axis=2
    )
    received = lax.all_to_all(packed, ("space", "sub"), 0, 0, tiled=True)
    sums = splat(received.reshape(devices * tiles_each, 8, slot_total))
    grid = to_grid(sums)
    density_field = grid[3]

    h0 = HALO0
    g = exchange(grid, h0, 1, 2)
    vx, vy, vz, rho0 = g[0], g[1], g[2], g[3]
    mask0 = inside_mask(CX, CY, CZ, h0)
    hf = h0 - 1
    vzc = jnp.pad(crop(vz, h0, hf), ((0, 0), (0, 0), (1, 1)))
    change = vx[2:, 1:-1] - vx[:-2, 1:-1] + (vy[1:-1, 2:] - vy[1:-1, :-2])
    change = change + (vzc[:, :, 2:] - vzc[:, :, :-2])
    m0 = crop(mask0, h0, hf)
    f0 = -0.5 * change * m0
    screen0 = screen_weight * crop(rho0, h0, hf)
    diag0 = 6.0 + screen0
    u = relax_weight * f0 / diag0 * m0
    u = sweep_ext(u, hf, f0, screen0, diag0, m0, 1.0)
    hu0 = hf - 1
    residual0 = crop(f0, hf, 0) - operate_ext(
        crop(u, hu0, 1), crop(screen0, hf, 0), 1.0
    )

    h1 = HALO1
    f1 = restrict(residual0)
    rho1 = restrict(density_field)
    nx1, ny1, nz1 = f1.shape
    both = exchange(jnp.stack([f1, rho1]), h1, 1, 2)
    f1e, rho1e = both[0], both[1]
    mask1 = inside_mask(nx1, ny1, nz1, h1)
    scale1 = 0.25
    screen1 = screen_weight * rho1e
    diag1 = 6.0 * scale1 + screen1
    u1 = relax_weight * f1e / diag1 * mask1
    u1 = sweep_ext(u1, h1, f1e, screen1, diag1, mask1, scale1)
    hu1 = h1 - 1
    residual1 = crop(f1e, h1, 0) - operate_ext(crop(u1, hu1, 1), crop(screen1, h1, 0), scale1)

    f2 = restrict(residual1)
    rho2 = restrict(rho1)
    nx2, ny2, nz2 = f2.shape

    def gather(x):
        every = lax.all_gather(x, ("space", "sub"), axis=0, tiled=False)
        every = every.reshape(space_count, sub_count, nx2, ny2, nz2)
        return every.transpose(0, 2, 1, 3, 4).reshape(space_count * nx2, sub_count * ny2, nz2)

    rho2g = gather(rho2)
    f2g = gather(f2)
    rho3g = restrict(rho2g)
    screens = [None, None, screen_weight * rho2g, screen_weight * rho3g]
    c2g = vcycle_global(f2g, 2, screens)
    hc2 = (hu1 + 1) // 2
    c2p = jnp.pad(c2g, ((hc2, hc2), (hc2, hc2), (0, 0)))
    c2 = lax.dynamic_slice(
        c2p,
        (lax.axis_index("space") * nx2, lax.axis_index("sub") * ny2, 0),
        (nx2 + 2 * hc2, ny2 + 2 * hc2, nz2),
    )

    u1 = u1 + crop(prolong(c2), 2 * hc2, hu1)
    hcur = hu1
    while hcur > 1:
        u1 = sweep_ext(
            u1,
            hcur,
            crop(f1e, h1, hcur),
            crop(screen1, h1, hcur),
            crop(diag1, h1, hcur),
            crop(mask1, h1, hcur),
            scale1,
        )
        hcur -= 1
    c1 = u1

    u = u + crop(prolong(c1), 2, hu0)
    hcur = hu0
    for _ in range(SWEEPS):
        u = sweep_ext(
            u,
            hcur,
            crop(f0, hf, hcur),
            crop(screen0, hf, hcur),
            crop(diag0, hf, hcur),
            crop(m0, hf, hcur),
            1.0,
        )
        hcur -= 1
    indicator = crop(u, hcur, 0)
    return (indicator, density_field)


def solution(mesh):
    placed = (
        P("space", "sub", None, None, None, None, None),
        P("space", "sub", None, None, None, None, None),
        P("space", "sub", None, None, None, None),
        P("space", "sub", None, None, None),
        P("space", "sub", None, None, None),
    )
    return jax.shard_map(
        on_device,
        mesh=mesh,
        in_specs=placed,
        out_specs=(P("space", "sub", None), P("space", "sub", None)),
        check_vma=False,
    )
```

time: 892 us -> 573 us (0.64)
  the two profiles are of different devices: /device:TPU:14 before, /device:TPU:1 now
where the time goes in v1:
time: 573 us
  local copies, waits for them, and re-layouts  143 us (25%)
  blocking collectives  136 us (24%)
  waiting for transfers between devices  101 us (18%)
  matrix products  78.4 us (14%)
  other arithmetic  75.2 us (13%)
  starting transfers between devices  37.6 us (7%)
    all_gather x2, blocking collectives, gather(): every = lax.all_gather(x, ('space', 'sub'), axis=0, tiled=False)  136 us
    all_to_all x1, waiting for transfers between devices, on_device(): received = lax.all_to_all(packed, ('space', 'sub'), 0, 0, tiled=True)  95.9 us
    dot_general x1, matrix products, splat(): jnp.einsum('tas,tbs->tab', planar, loaded, precision=lax.Precision.HIGHEST)  69 us
    reshape x3, local copies, waits for them, and re-layouts, restrict(): field.reshape(sx // 2, 2, sy // 2, 2, sz // 2, 2).mean(axis=(1, 3, 5))  46 us
    reduce_sum x6, other arithmetic, restrict(): field.reshape(sx // 2, 2, sy // 2, 2, sz // 2, 2).mean(axis=(1, 3, 5))  32.8 us
    another operation x2, local copies, waits for them, and re-layouts, restrict(): field.reshape(sx // 2, 2, sy // 2, 2, sz // 2, 2).mean(axis=(1, 3, 5))  25.2 us
    convert_element_type x1, other arithmetic, splat(): bricks = packed[:, 7, 0].astype(jnp.int32)  20.4 us
    all_to_all x1, starting transfers between devices, on_device(): received = lax.all_to_all(packed, ('space', 'sub'), 0, 0, tiled=True)  17 us
  transfers between devices with their start and end apart: 9, of which 3 were waited for; matrix products, arithmetic and copies ran while one was open for 10% of the time, Pallas kernels for 0%

profile of v1, /device:TPU:1, one launch (start us, length us, event | category | flops | bytes accessed | tf_op | source)
XLA Modules:
  0.0 572.8 jit_solution(12029851106029640467)
XLA Ops:
  0.7 0.9 convert_element_type.69
  1.7 0.9 copy.190
  2.9 2.0 copy.148
  4.9 0.6 copy.149
  5.5 1.1 maximum_multiply_fusion
  6.6 1.2 broadcast_in_dim.37
  7.9 3.4 pad_maximum_fusion
  11.3 17.0 %all-to-all-start = ((f32[256,4,8,128]{3,2,1,0:T(8,128)}), f32[256,4,8,128]{3,2,1,0:T(8,128)}, u32[]{:S(2)}, u32[]{:S(2)}) async-start(f32[256,4,8,128]{3,2,1,0:T(8,128)} %pad_maximum_fusion), calls=%async_computation | async-start | bytes 8388608 | tf_op jit(solution)/shard_map/all_to_all | solution.py:161
  28.4 0.7 fusion.182
  29.3 95.9 %all-to-all-done = f32[256,4,8,128]{3,2,1,0:T(8,128)} async-done(((f32[256,4,8,128]{3,2,1,0:T(8,128)}), f32[256,4,8,128]{3,2,1,0:T(8,128)}, u32[]{:S(2)}, u32[]{:S(2)}) %all-to-all-start) | async-done | bytes 4194336 | tf_op jit(solution)/shard_map/all_to_all | solution.py:161
  125.2 20.4 %fusion.54 = s32[1024]{0:T(1024)S(1)} fusion(f32[1024,8,128]{2,1,0:T(8,128)} %bitcast.5), kind=kLoop, calls=%fused_computation.96 | loop fusion | flops 1024 | bytes 8192 | tf_op jit(solution)/shard_map/convert_element_type | solution.py:113
  145.6 2.6 slice.775
  148.2 2.5 slice.772
  150.8 6.6 %subtract_maximum_fusion = f32[1024,3,8,128]{3,2,0,1:T(8,128)} fusion(f32[8]{0:T(128)S(1)} %iota_add_fusion, f32[1024,3,128]{2,0,1:T(8,128)S(1)} %copy.154), kind=kLoop, calls=%fused_computation.7 | loop fusion | flops 12582912 | bytes 14155808 | tf_op jit(solution)/shard_map/max | solution.py:115
  157.4 9.4 %slice_bitcast_fusion = (f32[1024,8,128]{2,1,0:T(8,128)}, f32[1024,8,128]{2,1,0:T(8,128)}, f32[1024,8,128]{2,1,0:T(8,128)}) fusion(f32[1024,3,8,128]{3,2,0,1:T(8,128)} %subtract_maximum_fusion), kind=kLoop, calls=%fused_computation.10 | loop fusion | bytes 25165824 | tf_op jit(solution)/shard_map/mul | solution.py:119
  166.9 69.0 %fusion = f32[1024,64,32]{1,2,0:T(8,128)} fusion(f32[1024,8,128]{2,1,0:T(8,128)} %get-tuple-element.5, f32[1024,8,128]{2,1,0:T(8,128)} %get-tuple-element.6, f32[1024,8,128]{2,1,0:T(8,128)} %get-tuple-element.4, f32[1024,4,128]{2,1,0:T(4,128)S(1)} %slice.775), kind=kOutput, calls=%fused_computation | convolution fusion | flops 3233808384 | bytes 23068672 | tf_op jit(solution)/shard_map/tas,tbs->tab/dot_general | solution.py:122
  235.8 13.8 %copy.155 = f32[1024,64,32]{0,2,1:T(8,128)} copy(f32[1024,64,32]{1,2,0:T(8,128)} %fusion) | data formatting | bytes 16777216 | tf_op jit(solution)/shard_map/tas,tbs->tab/dot_general | solution.py:122
  249.7 9.4 %convolution_bitcast_fusion = f32[4,2,8,2,8,16,8]{5,6,0,4,2,3,1:T(8,128)S(1)} fusion(f32[8,8,4,8,1024,1,1]{4,3,2,1,0,6,5:T(8,128)} %bitcast.92, s32[2,2,16]{2,1,0:T(2,128)S(1)} %multiply_add_fusion, s32[1024]{0:T(1024)S(1)} %fusion.54), kind=kOutput, calls=%fused_computation.38 | convolution fusion | flops 1610678272 | bytes 8917248 | tf_op jit(solution)/shard_map/dot_general | solution.py:128
  259.1 2.0 copy-done.2
  261.1 7.1 %copy.156 = f32[4,2,8,2,8,16,8]{6,5,4,3,2,1,0:T(8,128)} copy(f32[4,2,8,2,8,16,8]{5,6,0,4,2,3,1:T(8,128)} %copy-done.2) | data formatting | bytes 1048576 | tf_op jit(solution)/shard_map/transpose | solution.py:135
  268.2 0.6 copy.157
  268.9 6.4 %reshape.187 = f32[4,16,16,128]{3,2,1,0:T(8,128)S(1)} reshape(f32[4,2,8,2,8,16,8]{6,5,4,3,2,1,0:T(8,128)} %copy.156) | data formatting | bytes 1048576 | tf_op jit(solution)/shard_map/reshape | solution.py:135
  275.2 0.8 fusion.221
  276.0 1.3 collective-permute-start.1
  277.3 4.7 collective-permute-start
  282.0 4.3 reshape_squeeze.3
  286.3 4.0 reduce_sum.55
  290.3 1.1 div.96
  291.6 0.9 constant_dynamic-update-slice_fusion.2
  292.5 1.1 constant_dynamic-update-slice_fusion.1
  293.6 0.9 constant_dynamic-update-slice_fusion
  294.6 4.5 collective-permute-start.2
  299.1 1.9 collective-permute-start.3
  301.0 0.7 collective-permute-done.2
  301.7 4.4 collective-permute-done.3
  307.1 0.7 copy-done.3
  307.9 9.8 %reshape.188 = f32[8,2,8,2,64,2]{5,4,3,2,1,0:T(8,128)} reshape(f32[16,16,128]{2,1,0:T(8,128)S(1)} %fusion.85) | data formatting | bytes 262144 | tf_op jit(solution)/shard_map/reshape | solution.py:70
  317.7 4.0 reduce_sum.54
  321.8 1.4 collective-permute-start.4
  323.2 1.3 collective-permute-start.5
  324.5 69.0 %all-gather.1 = f32[1024,4,32]{2,1,0:T(4,128)S(1)} all-gather(f32[4,4,32]{2,1,0:T(4,128)S(1)} %broadcast_multiply_fusion.2), channel_id=3, replica_groups=mesh['space'=32,'sub'=8] {'space','sub'}, dimensions={0}, use_global_device_ids=true | all-gather | bytes 526336 | tf_op jit(solution)/shard_map/all_gather | solution.py:205
  393.6 2.1 collective-permute-start.7
  395.6 3.5 collective-permute-start.6
  399.2 2.3 broadcast_multiply_fusion
  401.5 1.6 squeeze.25
  403.1 2.6 copy.203
  405.7 0.7 copy.173
  406.4 2.0 copy.167
  408.4 2.7 copy.168
  411.0 21.0 %reshape_reshape.3 = f32[64,2,16,2,16,2]{5,4,3,2,1,0:T(8,128)} reshape(f32[32,4,8,4,32]{4,3,2,1,0:T(4,128)S(1)} %copy.173) | data formatting | bytes 1048576 | tf_op jit(solution)/shard_map/reshape;reshape | solution.py:70
  432.0 12.3 %reduce_sum.59 = f32[64,16,16]{2,1,0:T(8,128)S(1)} reduce(f32[64,2,16,2,16,2]{5,4,3,2,1,0:T(8,128)} %reshape_reshape.3, f32[]{:T(128)} %constant.35.clone.1), dimensions={1,3,5}, to_apply=%region_5.6 | reduce | flops 114688 | bytes 589828 | tf_op jit(solution)/shard_map/reduce_sum | solution.py:70
  445.1 1.1 reshape.189
  446.4 66.9 %all-gather = f32[1024,4,32]{2,1,0:T(4,128)S(1)} all-gather(f32[4,4,32]{2,1,0:T(4,128)S(1)} %broadcast_multiply_fusion.3), channel_id=2, replica_groups=mesh['space'=32,'sub'=8] {'space','sub'}, dimensions={0}, use_global_device_ids=true | all-gather | bytes 526336 | tf_op jit(solution)/shard_map/all_gather | solution.py:205
  513.4 1.8 copy.163
  515.2 1.3 copy.164
  516.6 0.5 fusion.20
  517.5 35.1 %reshape.193 = f32[64,2,16,2,16,2]{1,0,5,4,3,2:T(8,128)} reshape(f32[128,32,32]{0,2,1:T(8,128)S(1)} %fusion.29) | data formatting | bytes 1048576 | tf_op jit(solution)/shard_map/reshape | solution.py:70
  552.6 12.2 %reduce_sum.58 = f32[64,16,16]{0,2,1:T(8,128)S(1)} reduce(f32[64,2,16,2,16,2]{1,0,5,4,3,2:T(8,128)} %reshape.193, f32[]{:T(128)} %constant.35.clone.1), dimensions={1,3,5}, to_apply=%region_4.5 | reduce | flops 114688 | bytes 589828 | tf_op jit(solution)/shard_map/reduce_sum | solution.py:70
  566.5 0.4 copy.176
  567.5 0.5 fusion.41
  568.0 0.5 fusion.53
  570.4 0.5 broadcast_in_dim.46
  570.9 0.4 copy.186
  571.7 0.8 fusion.94
  (131 shorter events, 8.1 us)
Async XLA Ops:
  0.6 4.2 copy-start.16
  0.6 4.8 copy-start.23
  11.3 114.0 %all-to-all-start = ((f32[256,4,8,128]{3,2,1,0:T(8,128)}), f32[256,4,8,128]{3,2,1,0:T(8,128)}, u32[]{:S(2)}, u32[]{:S(2)}) async-start(f32[256,4,8,128]{3,2,1,0:T(8,128)} %pad_maximum_fusion), calls=%async_computation | async-start | bytes 8388608 | tf_op jit(solution)/shard_map/all_to_all | solution.py:161
  29.3 277.4 %copy-start.5 = (f32[24,24,128]{2,1,0:T(8,128)}, f32[24,24,128]{2,1,0:T(8,128)S(1)}, u32[]{:S(2)}) copy-start(f32[24,24,128]{2,1,0:T(8,128)S(1)} %and_convert_fusion) | copy-start | bytes 884740
  259.1 2.0 copy-start.2
  261.1 7.1 %slice-start = ((f32[4,2,8,2,8,16,8]{5,6,0,4,2,3,1:T(8,128)}), f32[1,2,8,2,8,16,8]{5,6,0,4,2,3,1:T(8,128)S(1)}, s32[]{:S(2)}) async-start(f32[4,2,8,2,8,16,8]{5,6,0,4,2,3,1:T(8,128)} %copy-done.2), calls=%async_computation.1 | async-start | bytes 2097152 | tf_op jit(solution)/shard_map/slice | solution.py:164
  275.2 11.0 %copy-start.11 = (f32[4,16,16,128]{3,2,1,0:T(8,128)}, f32[4,16,16,128]{3,2,1,0:T(8,128)S(1)}, u32[]{:S(2)}) copy-start(f32[4,16,16,128]{3,2,1,0:T(8,128)S(1)} %reshape.187) | copy-start | bytes 1572868
  276.0 17.5 %collective-permute-start.1 = (f32[4,4,16,128]{3,2,1,0:T(8,128)}, f32[4,4,16,128]{3,2,1,0:T(8,128)}, u32[]{:S(2)}, u32[]{:S(2)}) collective-permute-start(f32[4,4,16,128]{3,2,1,0:T(8,128)} %get-tuple-element.13), channel_id=1, source_target_pairs={{8,0},{16,8},{24,16},{32,24},{40,32},{48,40},{56,48},{64,56},{72,6... | collective-permute-start | bytes 393224 | tf_op jit(solution)/shard_map/ppermute | solution.py:30
  277.3 14.2 %collective-permute-start = (f32[4,4,16,128]{3,2,1,0:T(8,128)}, f32[4,4,16,128]{3,2,1,0:T(8,128)}, u32[]{:S(2)}, u32[]{:S(2)}) collective-permute-start(f32[4,4,16,128]{3,2,1,0:T(8,128)} %get-tuple-element.14), channel_id=1, source_target_pairs={{0,8},{8,16},{16,24},{24,32},{32,40},{40,48},{48,56},{56,64},{64,7... | collective-permute-start | bytes 393224 | tf_op jit(solution)/shard_map/ppermute | solution.py:29
  294.6 7.1 %collective-permute-start.2 = (f32[4,24,4,128]{3,2,1,0:T(4,128)S(1)}, f32[4,24,4,128]{3,2,1,0:T(4,128)S(1)}, u32[]{:S(2)}, u32[]{:S(2)}) collective-permute-start(f32[4,24,4,128]{3,2,1,0:T(4,128)S(1)} %get-tuple-element.11), channel_id=1, source_target_pairs={{0,1},{1,2},{2,3},{3,4},{4,5},{5,6},{6,7},{8,9},{9,10},{10,11},{11... | collective-permute-start | bytes 589832 | tf_op jit(solution)/shard_map/ppermute | solution.py:29
  299.1 7.0 %collective-permute-start.3 = (f32[4,24,4,128]{3,2,1,0:T(4,128)S(1)}, f32[4,24,4,128]{3,2,1,0:T(4,128)S(1)}, u32[]{:S(2)}, u32[]{:S(2)}) collective-permute-start(f32[4,24,4,128]{3,2,1,0:T(4,128)S(1)} %get-tuple-element.12), channel_id=1, source_target_pairs={{1,0},{2,1},{3,2},{4,3},{5,4},{6,5},{7,6},{9,8},{10,9},{11,10},{12... | collective-permute-start | bytes 589832 | tf_op jit(solution)/shard_map/ppermute | solution.py:30
  306.7 11.0 %copy-start.7 = (f32[22,22,128]{2,1,0:T(8,128)}, f32[22,22,128]{2,1,0:T(8,128)S(1)}, u32[]{:S(2)}) copy-start(f32[22,22,128]{2,1,0:T(8,128)S(1)} %get-tuple-element.15) | copy-start | bytes 743428
  306.7 11.0 %copy-start.9 = (f32[22,22,128]{2,1,0:T(8,128)}, f32[22,22,128]{2,1,0:T(8,128)S(1)}, u32[]{:S(2)}) copy-start(f32[22,22,128]{2,1,0:T(8,128)S(1)} %get-tuple-element.18) | copy-start | bytes 743428
  306.7 11.0 %copy-start.12 = (f32[22,22,128]{2,1,0:T(8,128)}, f32[22,22,128]{2,1,0:T(8,128)S(1)}, u32[]{:S(2)}) copy-start(f32[22,22,128]{2,1,0:T(8,128)S(1)} %get-tuple-element.16) | copy-start | bytes 743428
  307.1 0.7 copy-start.3
  321.8 71.7 %collective-permute-start.4 = (f32[2,4,8,64]{3,2,1,0:T(8,128)S(1)}, f32[2,4,8,64]{3,2,1,0:T(8,128)S(1)}, u32[]{:S(2)}, u32[]{:S(2)}) collective-permute-start(f32[2,4,8,64]{3,2,1,0:T(8,128)S(1)} %get-tuple-element.25), channel_id=1, source_target_pairs={{0,8},{8,16},{16,24},{24,32},{32,40},{40,48},{48,56},{56,64},{64,7... | collective-permute-start | bytes 49160 | tf_op jit(solution)/shard_map/ppermute | solution.py:29
  323.2 70.3 %collective-permute-start.5 = (f32[2,4,8,64]{3,2,1,0:T(8,128)S(1)}, f32[2,4,8,64]{3,2,1,0:T(8,128)S(1)}, u32[]{:S(2)}, u32[]{:S(2)}) collective-permute-start(f32[2,4,8,64]{3,2,1,0:T(8,128)S(1)} %get-tuple-element.26), channel_id=1, source_target_pairs={{8,0},{16,8},{24,16},{32,24},{40,32},{48,40},{56,48},{64,56},{72,6... | collective-permute-start | bytes 49160 | tf_op jit(solution)/shard_map/ppermute | solution.py:30
  393.5 5.7 copy-start
  393.6 50.9 %collective-permute-start.7 = (f32[2,16,4,64]{3,1,2,0:T(8,128)S(1)}, f32[2,16,4,64]{3,1,2,0:T(8,128)S(1)}, u32[]{:S(2)}, u32[]{:S(2)}) collective-permute-start(f32[2,16,4,64]{3,1,2,0:T(8,128)S(1)} %copy.197), channel_id=1, source_target_pairs={{1,0},{2,1},{3,2},{4,3},{5,4},{6,5},{7,6},{9,8},{10,9},{11,10},{12... | collective-permute-start | bytes 98312 | tf_op jit(solution)/shard_map/ppermute | solution.py:30
  395.6 48.9 %collective-permute-start.6 = (f32[2,16,4,64]{3,1,2,0:T(8,128)S(1)}, f32[2,16,4,64]{3,1,2,0:T(8,128)S(1)}, u32[]{:S(2)}, u32[]{:S(2)}) collective-permute-start(f32[2,16,4,64]{3,1,2,0:T(8,128)S(1)} %copy.196), channel_id=1, source_target_pairs={{0,1},{1,2},{2,3},{3,4},{4,5},{5,6},{6,7},{8,9},{9,10},{10,11},{11... | collective-permute-start | bytes 98312 | tf_op jit(solution)/shard_map/ppermute | solution.py:29
  403.1 3.3 copy-start.1
  432.0 12.9 %copy-start.19 = (f32[16,16,64]{2,1,0:T(8,128)S(1)}, f32[16,16,64]{2,1,0:T(8,128)}, u32[]{:S(2)}) copy-start(f32[16,16,64]{2,1,0:T(8,128)} %fusion.182) | copy-start | bytes 196612
  444.7 68.6 %copy-start.17 = (f32[16,16,64]{2,1,0:T(8,128)}, f32[16,16,64]{2,1,0:T(8,128)S(1)}, u32[]{:S(2)}) copy-start(f32[16,16,64]{2,1,0:T(8,128)S(1)} %get-tuple-element.21) | copy-start | bytes 196612
  444.8 68.6 %copy-start.14 = (f32[16,16,64]{2,1,0:T(8,128)}, f32[16,16,64]{2,1,0:T(8,128)S(1)}, u32[]{:S(2)}) copy-start(f32[16,16,64]{2,1,0:T(8,128)S(1)} %get-tuple-element.20) | copy-start | bytes 196612
  445.0 68.4 %copy-start.21 = (f32[14,14,64]{2,1,0:T(8,128)}, f32[14,14,64]{2,1,0:T(8,128)S(1)}, u32[]{:S(2)}) copy-start(f32[14,14,64]{2,1,0:T(8,128)S(1)} %slice_multiply_fusion.4) | copy-start | bytes 150532
  567.5 2.0 copy-start.22
  567.5 2.0 copy-start.15
  567.5 2.0 copy-start.18
  567.5 2.0 copy-start.20
  569.2 2.1 copy-start.4
  569.5 1.8 copy-start.6
  569.5 1.8 copy-start.8
  569.5 1.8 copy-start.10
  569.5 1.8 copy-start.13
